TPU v7x, 32 devices: a whole 2x2x4 slice. The times are simulated.
32 devices in a mesh: job: 2 (over x), space: 4 (over y, core), arc: 4 (over z).
Axes of the slice: x: 2, y: 2, z: 4, core: 2. Of those that a mesh axis runs over, the one named last changes fastest.
Arguments:
- saved_velocity_trajectory: bfloat16 [64, 3, 8, 128, 128], P(('job', 'arc'), None, 'space'), parts along dimension 0, may hold values from -4 to 4
- saved_warmth_trajectory: bfloat16 [64, 8, 128, 128], P(('job', 'arc'), 'space'), parts along dimension 0, may hold values from -5 to 5
- control_porosity: float32 [16, 128, 128], P(('job', 'space')), parts along dimension 0, may hold values from 0.05 to 1
- control_volume_flag: int32 [16, 128, 128], P(('job', 'space')), parts along dimension 0, may hold values 0 or 1
- entrance_face_flag: int32 [256, 128], P('job'), parts along dimension 0, may hold values 0 or 1
Outputs:
- gradient: float32 [16, 128, 128], P(('job', 'space'), 'arc'), parts along dimension 0
- entry_adjoint: float32 [8, 4, 8, 128, 128], P(('job', 'arc'), None, 'space'), parts along dimension 0
There are 2 independent parts, one for each index of `job`. A program takes and returns all parts, laid end to end along the dimension named above; each array names one. Nothing has to cross between parts.
All inputs are finite; a program needn't handle non-finite values. No bound on the sum of `control_volume_flag` on one device may be relied on, other than what follows from the above.
Results may differ from a plain program's by a relative error of at most 0.0003.
Values may be sent and summed in bfloat16 or wider, within the bound.
No kernel may reach another device: no remote copies, remote signals or barrier semaphores. Data moves between devices by JAX's collectives and lax.ppermute only.
A program may use at most 64 MiB of HBM per device.

v0:
```python
import jax
import jax.numpy as jnp
from jax import lax
from jax.sharding import PartitionSpec as P


def padded(cells, sides, width):
    for axis, dim in sides:
        count = lax.axis_size(axis)
        ends = count - 1
        head = lax.slice_in_dim(cells, 0, width, axis=dim)
        tail = lax.slice_in_dim(cells, cells.shape[dim] - width, cells.shape[dim], axis=dim)
        cells = jnp.concatenate(
            [
                lax.ppermute(tail, axis, [(i, (i + 1) % count) for i in range(ends)]),
                cells,
                lax.ppermute(head, axis, [((i + 1) % count, i) for i in range(ends)]),
            ],
            axis=dim,
        )
    return cells


def passed_along(value, axis, steps):
    count = lax.axis_size(axis)
    pairs = [(source, (source + steps) % count) for source in range(count)]
    return lax.ppermute(value, axis, pairs)


def laplace(ext):
    mid = ext[..., 1:-1, 1:-1, 1:-1]
    total = ext[..., 2:, 1:-1, 1:-1] + ext[..., :-2, 1:-1, 1:-1]
    total = total + ext[..., 1:-1, 2:, 1:-1] + ext[..., 1:-1, :-2, 1:-1]
    total = total + ext[..., 1:-1, 1:-1, 2:] + ext[..., 1:-1, 1:-1, :-2]
    return total - 6.0 * mid


def slopes(ext):
    return (
        0.5 * (ext[..., 2:, 1:-1, 1:-1] - ext[..., :-2, 1:-1, 1:-1]),
        0.5 * (ext[..., 1:-1, 2:, 1:-1] - ext[..., 1:-1, :-2, 1:-1]),
        0.5 * (ext[..., 1:-1, 1:-1, 2:] - ext[..., 1:-1, 1:-1, :-2]),
    )


def pad_sides(field, operating_variant):
    widths = [(0, 0)] * (field.ndim - 2) + [(1, 1), (1, 1)]
    return jnp.pad(field, widths, mode=operating_variant)


def adjoint_update(
    adj,
    ext_a,
    ext_b,
    padded_thermal_field,
    speed,
    alpha,
    porosity_sensitivity,
    solid,
    quadrature_factor,
):
    a_now = adj[:3]
    current_adjoint_vector = adj[3]
    grad_b = slopes(ext_b)
    grad_a = slopes(ext_a)
    grad_t = slopes(padded_thermal_field)
    carry_b = speed[0] * grad_b[0] + speed[1] * grad_b[1] + speed[2] * grad_b[2]
    carry_a = speed[0:1] * grad_a[0] + speed[1:2] * grad_a[1] + speed[2:3] * grad_a[2]
    thermal_current_field = padded_thermal_field[1:-1, 1:-1, 1:-1]
    grad_stack = jnp.stack(grad_t)
    new_a = a_now + 0.1 * (
        1.2 * laplace(ext_a) + carry_a - alpha * a_now - current_adjoint_vector * grad_stack
    )
    new_b = current_adjoint_vector + 0.1 * (
        1.2 * laplace(ext_b) + carry_b - 2.0 * solid * current_adjoint_vector + 2.0 * solid
    )
    common_divisor_lcm_like = jnp.sum(a_now * speed, axis=0)
    summand_contribution = (
        0.1
        * quadrature_factor
        * (
            porosity_sensitivity * common_divisor_lcm_like
            + 2.0 * (current_adjoint_vector - 1.0) * thermal_current_field
        )
    )
    return (jnp.concatenate([new_a, new_b[None]], axis=0), summand_contribution)


def body(
    saved_velocity_trajectory,
    saved_warmth_trajectory,
    control_porosity,
    control_volume_flag,
    entrance_face_flag,
):
    quadrature_factor = control_volume_flag.astype(jnp.float32)
    gamma = jnp.where(control_volume_flag == 1, control_porosity, jnp.float32(0.0))
    solid = 1.0 - gamma
    alpha = 3.0 * 0.1 * solid / (0.1 + gamma)
    porosity_sensitivity = -3.0 * 0.1 * 1.1 / ((0.1 + gamma) * (0.1 + gamma))
    leading_plane = lax.axis_index("space") == 0
    trailing_plane = lax.axis_index("space") == lax.axis_size("space") - 1
    device_instant_total = saved_warmth_trajectory.shape[0]
    cycle_ext = padded(saved_warmth_trajectory, (("space", 1),), 1)

    def closing_thermal_value(thermal_current_field, with_halo_padding):
        floor_limit = jnp.where(leading_plane, thermal_current_field[0], with_halo_padding[0])
        ceiling_bound = jnp.where(trailing_plane, thermal_current_field[-1], with_halo_padding[-1])
        return pad_sides(
            jnp.concatenate(
                [floor_limit[None], thermal_current_field, ceiling_bound[None]], axis=0
            ),
            "edge",
        )

    def one_step(adj, interior_block):
        speed = saved_velocity_trajectory[interior_block].astype(jnp.float32)
        thermal_current_field = saved_warmth_trajectory[interior_block].astype(jnp.float32)
        with_halo_padding = padded(adj, (("space", 1),), 1)
        thermal_halo_values = cycle_ext[interior_block].astype(jnp.float32)
        complete_thermal_field = jnp.concatenate(
            [thermal_halo_values[:1], thermal_current_field, thermal_halo_values[-1:]], axis=0
        )
        padded_thermal_field = closing_thermal_value(thermal_current_field, complete_thermal_field)
        ext_a = pad_sides(with_halo_padding[:3], "constant")
        current_adjoint_vector = adj[3]
        floor_limit = jnp.where(
            leading_plane,
            jnp.where(entrance_face_flag == 1, jnp.float32(0.0), current_adjoint_vector[0]),
            with_halo_padding[3, 0],
        )
        ceiling_bound = jnp.where(
            trailing_plane, current_adjoint_vector[-1], with_halo_padding[3, -1]
        )
        ext_b = pad_sides(
            jnp.concatenate(
                [floor_limit[None], current_adjoint_vector, ceiling_bound[None]], axis=0
            ),
            "edge",
        )
        return adjoint_update(
            adj,
            ext_a,
            ext_b,
            padded_thermal_field,
            speed,
            alpha,
            porosity_sensitivity,
            solid,
            quadrature_factor,
        )

    grid_shape = (4,) + control_porosity.shape
    adj = jnp.zeros(grid_shape, jnp.float32)
    for interior_block in range(device_instant_total - 1, -1, -1):
        adj, unused = one_step(adj, interior_block)
    adj = passed_along(adj, "arc", -1)
    partial_sum = jnp.zeros(control_porosity.shape, jnp.float32)
    for interior_block in range(device_instant_total - 1, -1, -1):
        adj, summand_contribution = one_step(adj, interior_block)
        partial_sum = partial_sum + summand_contribution
    summed = lax.psum(partial_sum, "arc")
    share = summed.shape[1] // lax.axis_size("arc")
    gradient = lax.dynamic_slice_in_dim(summed, lax.axis_index("arc") * share, share, 1)
    return (gradient, adj[None])


def solution(mesh):
    return jax.shard_map(
        body,
        mesh=mesh,
        in_specs=(
            P(("job", "arc"), None, "space", None, None),
            P(("job", "arc"), "space", None, None),
            P(("job", "space"), None, None),
            P(("job", "space"), None, None),
            P("job", None),
        ),
        out_specs=(P(("job", "space"), "arc", None), P(("job", "arc"), None, "space", None, None)),
        check_vma=False,
    )
```

profile of v0, /device:TPU:0, one launch (start us, length us, event | category | flops | bytes accessed | tf_op | source)
XLA Modules:
  0.0 265.9 jit_solution(15857158346192255144)
XLA Ops:
  9.4 3.8 %collective-permute-start.1 = (f32[4,1,128,128]{3,2,1,0:T(8,128)}, f32[4,1,128,128]{3,2,1,0:T(8,128)}, u32[]{:S(2)}, u32[]{:S(2)}) collective-permute-start(f32[4,1,128,128]{3,2,1,0:T(8,128)} %broadcast.302), channel_id=1, source_target_pairs={{0,4},{4,8},{8,12},{1,5},{5,9},{9,13},{2,6},{6,10},{10,14},{3,7},{... | collective-permute-start | bytes 786440 | tf_op jit(solution)/shard_map/ppermute | solution.py:15
  15.0 4.5 %collective-permute-start.2 = (bf16[8,1,128,128]{3,2,1,0:T(8,128)(2,1)}, bf16[8,1,128,128]{3,2,1,0:T(8,128)(2,1)}, u32[]{:S(2)}, u32[]{:S(2)}) collective-permute-start(bf16[8,1,128,128]{3,2,1,0:T(8,128)(2,1)} %get-tuple-element.84), channel_id=1, source_target_pairs={{0,4},{4,8},{8,12},{1,5},{5,9},{9,13},{2,6},{6,10},{10,14},{3,7},{... | collective-permute-start | bytes 786440 | tf_op jit(solution)/shard_map/ppermute | solution.py:15
  41.1 3.7 %collective-permute-start.5 = (f32[4,1,128,128]{3,2,1,0:T(8,128)S(1)}, f32[4,1,128,128]{3,2,1,0:T(8,128)S(1)}, u32[]{:S(2)}, u32[]{:S(2)}) collective-permute-start(f32[4,1,128,128]{3,2,1,0:T(8,128)S(1)} %get-tuple-element.81), channel_id=1, source_target_pairs={{0,4},{4,8},{8,12},{1,5},{5,9},{9,13},{2,6},{6,10},{10,14},{3,7},{... | collective-permute-start | bytes 786440 | tf_op jit(solution)/shard_map/ppermute | solution.py:15
  49.5 6.4 %collective-permute-start.7 = (f32[4,1,128,128]{3,2,1,0:T(8,128)S(1)}, f32[4,1,128,128]{3,2,1,0:T(8,128)S(1)}, u32[]{:S(2)}, u32[]{:S(2)}) collective-permute-start(f32[4,1,128,128]{3,2,1,0:T(8,128)S(1)} %get-tuple-element.79), channel_id=1, source_target_pairs={{0,4},{4,8},{8,12},{1,5},{5,9},{9,13},{2,6},{6,10},{10,14},{3,7},{... | collective-permute-start | bytes 786440 | tf_op jit(solution)/shard_map/ppermute | solution.py:15
  59.1 6.6 %collective-permute-start.9 = (f32[4,1,128,128]{3,2,1,0:T(8,128)S(1)}, f32[4,1,128,128]{3,2,1,0:T(8,128)S(1)}, u32[]{:S(2)}, u32[]{:S(2)}) collective-permute-start(f32[4,1,128,128]{3,2,1,0:T(8,128)S(1)} %get-tuple-element.77), channel_id=1, source_target_pairs={{0,4},{4,8},{8,12},{1,5},{5,9},{9,13},{2,6},{6,10},{10,14},{3,7},{... | collective-permute-start | bytes 786440 | tf_op jit(solution)/shard_map/ppermute | solution.py:15
  67.3 3.9 %collective-permute-done.8 = f32[4,1,128,128]{3,2,1,0:T(8,128)S(1)} collective-permute-done((f32[4,1,128,128]{3,2,1,0:T(8,128)S(1)}, f32[4,1,128,128]{3,2,1,0:T(8,128)S(1)}, u32[]{:S(2)}, u32[]{:S(2)}) %collective-permute-start.8) | collective-permute-done | bytes 262176 | tf_op jit(solution)/shard_map/ppermute | solution.py:17
  73.2 6.7 %collective-permute-start.11 = (f32[4,1,128,128]{3,2,1,0:T(8,128)S(1)}, f32[4,1,128,128]{3,2,1,0:T(8,128)S(1)}, u32[]{:S(2)}, u32[]{:S(2)}) collective-permute-start(f32[4,1,128,128]{3,2,1,0:T(8,128)S(1)} %get-tuple-element.75), channel_id=1, source_target_pairs={{0,4},{4,8},{8,12},{1,5},{5,9},{9,13},{2,6},{6,10},{10,14},{3,7},{... | collective-permute-start | bytes 786440 | tf_op jit(solution)/shard_map/ppermute | solution.py:15
  85.6 6.4 %collective-permute-start.13 = (f32[4,1,128,128]{3,2,1,0:T(8,128)S(1)}, f32[4,1,128,128]{3,2,1,0:T(8,128)S(1)}, u32[]{:S(2)}, u32[]{:S(2)}) collective-permute-start(f32[4,1,128,128]{3,2,1,0:T(8,128)S(1)} %get-tuple-element.73), channel_id=1, source_target_pairs={{0,4},{4,8},{8,12},{1,5},{5,9},{9,13},{2,6},{6,10},{10,14},{3,7},{... | collective-permute-start | bytes 786440 | tf_op jit(solution)/shard_map/ppermute | solution.py:15
  97.5 6.2 %collective-permute-start.15 = (f32[4,1,128,128]{3,2,1,0:T(8,128)S(1)}, f32[4,1,128,128]{3,2,1,0:T(8,128)S(1)}, u32[]{:S(2)}, u32[]{:S(2)}) collective-permute-start(f32[4,1,128,128]{3,2,1,0:T(8,128)S(1)} %get-tuple-element.71), channel_id=1, source_target_pairs={{0,4},{4,8},{8,12},{1,5},{5,9},{9,13},{2,6},{6,10},{10,14},{3,7},{... | collective-permute-start | bytes 786440 | tf_op jit(solution)/shard_map/ppermute | solution.py:15
  109.2 6.2 %collective-permute-start.17 = (f32[4,1,128,128]{3,2,1,0:T(8,128)S(1)}, f32[4,1,128,128]{3,2,1,0:T(8,128)S(1)}, u32[]{:S(2)}, u32[]{:S(2)}) collective-permute-start(f32[4,1,128,128]{3,2,1,0:T(8,128)S(1)} %get-tuple-element.69), channel_id=1, source_target_pairs={{0,4},{4,8},{8,12},{1,5},{5,9},{9,13},{2,6},{6,10},{10,14},{3,7},{... | collective-permute-start | bytes 786440 | tf_op jit(solution)/shard_map/ppermute | solution.py:15
  121.1 3.7 %collective-permute-start.18 = (f32[4,2,128,128]{3,2,1,0:T(8,128)S(1)}, f32[4,2,128,128]{3,2,1,0:T(8,128)S(1)}, u32[]{:S(2)}, u32[]{:S(2)}) collective-permute-start(f32[4,2,128,128]{3,2,1,0:T(8,128)S(1)} %pad_maximum_fusion.2), channel_id=1, source_target_pairs={{0,3},{1,0},{2,1},{3,2},{4,7},{5,4},{6,5},{7,6},{8,11},{9,8},{10,9... | collective-permute-start | bytes 1572872 | tf_op jit(solution)/shard_map/ppermute | solution.py:27
  124.8 9.0 %collective-permute-done.18 = f32[4,2,128,128]{3,2,1,0:T(8,128)S(1)} collective-permute-done((f32[4,2,128,128]{3,2,1,0:T(8,128)S(1)}, f32[4,2,128,128]{3,2,1,0:T(8,128)S(1)}, u32[]{:S(2)}, u32[]{:S(2)}) %collective-permute-start.18) | collective-permute-done | bytes 524320 | tf_op jit(solution)/shard_map/ppermute | solution.py:27
  133.8 5.3 %collective-permute-start.20 = (f32[4,1,128,128]{3,2,1,0:T(8,128)S(1)}, f32[4,1,128,128]{3,2,1,0:T(8,128)S(1)}, u32[]{:S(2)}, u32[]{:S(2)}) collective-permute-start(f32[4,1,128,128]{3,2,1,0:T(8,128)S(1)} %get-tuple-element.51), channel_id=1, source_target_pairs={{0,4},{4,8},{8,12},{1,5},{5,9},{9,13},{2,6},{6,10},{10,14},{3,7},{... | collective-permute-start | bytes 786440 | tf_op jit(solution)/shard_map/ppermute | solution.py:15
  144.1 6.2 %collective-permute-start.22 = (f32[4,1,128,128]{3,2,1,0:T(8,128)S(1)}, f32[4,1,128,128]{3,2,1,0:T(8,128)S(1)}, u32[]{:S(2)}, u32[]{:S(2)}) collective-permute-start(f32[4,1,128,128]{3,2,1,0:T(8,128)S(1)} %get-tuple-element.49), channel_id=1, source_target_pairs={{0,4},{4,8},{8,12},{1,5},{5,9},{9,13},{2,6},{6,10},{10,14},{3,7},{... | collective-permute-start | bytes 786440 | tf_op jit(solution)/shard_map/ppermute | solution.py:15
  151.7 2.1 collective-permute-done.21
  155.3 6.2 %collective-permute-start.24 = (f32[4,1,128,128]{3,2,1,0:T(8,128)S(1)}, f32[4,1,128,128]{3,2,1,0:T(8,128)S(1)}, u32[]{:S(2)}, u32[]{:S(2)}) collective-permute-start(f32[4,1,128,128]{3,2,1,0:T(8,128)S(1)} %get-tuple-element.47), channel_id=1, source_target_pairs={{0,4},{4,8},{8,12},{1,5},{5,9},{9,13},{2,6},{6,10},{10,14},{3,7},{... | collective-permute-start | bytes 786440 | tf_op jit(solution)/shard_map/ppermute | solution.py:15
  162.8 2.1 collective-permute-done.23
  166.4 6.2 %collective-permute-start.26 = (f32[4,1,128,128]{3,2,1,0:T(8,128)S(1)}, f32[4,1,128,128]{3,2,1,0:T(8,128)S(1)}, u32[]{:S(2)}, u32[]{:S(2)}) collective-permute-start(f32[4,1,128,128]{3,2,1,0:T(8,128)S(1)} %get-tuple-element.45), channel_id=1, source_target_pairs={{0,4},{4,8},{8,12},{1,5},{5,9},{9,13},{2,6},{6,10},{10,14},{3,7},{... | collective-permute-start | bytes 786440 | tf_op jit(solution)/shard_map/ppermute | solution.py:15
  177.6 6.2 %collective-permute-start.28 = (f32[4,1,128,128]{3,2,1,0:T(8,128)S(1)}, f32[4,1,128,128]{3,2,1,0:T(8,128)S(1)}, u32[]{:S(2)}, u32[]{:S(2)}) collective-permute-start(f32[4,1,128,128]{3,2,1,0:T(8,128)S(1)} %get-tuple-element.43), channel_id=1, source_target_pairs={{0,4},{4,8},{8,12},{1,5},{5,9},{9,13},{2,6},{6,10},{10,14},{3,7},{... | collective-permute-start | bytes 786440 | tf_op jit(solution)/shard_map/ppermute | solution.py:15
  188.7 6.2 %collective-permute-start.30 = (f32[4,1,128,128]{3,2,1,0:T(8,128)S(1)}, f32[4,1,128,128]{3,2,1,0:T(8,128)S(1)}, u32[]{:S(2)}, u32[]{:S(2)}) collective-permute-start(f32[4,1,128,128]{3,2,1,0:T(8,128)S(1)} %get-tuple-element.41), channel_id=1, source_target_pairs={{0,4},{4,8},{8,12},{1,5},{5,9},{9,13},{2,6},{6,10},{10,14},{3,7},{... | collective-permute-start | bytes 786440 | tf_op jit(solution)/shard_map/ppermute | solution.py:15
  199.8 6.2 %collective-permute-start.32 = (f32[4,1,128,128]{3,2,1,0:T(8,128)S(1)}, f32[4,1,128,128]{3,2,1,0:T(8,128)S(1)}, u32[]{:S(2)}, u32[]{:S(2)}) collective-permute-start(f32[4,1,128,128]{3,2,1,0:T(8,128)S(1)} %get-tuple-element.39), channel_id=1, source_target_pairs={{0,4},{4,8},{8,12},{1,5},{5,9},{9,13},{2,6},{6,10},{10,14},{3,7},{... | collective-permute-start | bytes 786440 | tf_op jit(solution)/shard_map/ppermute | solution.py:15
  207.4 2.1 collective-permute-done.31
  213.1 6.2 %collective-permute-start.34 = (f32[4,1,128,128]{3,2,1,0:T(8,128)S(1)}, f32[4,1,128,128]{3,2,1,0:T(8,128)S(1)}, u32[]{:S(2)}, u32[]{:S(2)}) collective-permute-start(f32[4,1,128,128]{3,2,1,0:T(8,128)S(1)} %get-tuple-element.37), channel_id=1, source_target_pairs={{0,4},{4,8},{8,12},{1,5},{5,9},{9,13},{2,6},{6,10},{10,14},{3,7},{... | collective-permute-start | bytes 786440 | tf_op jit(solution)/shard_map/ppermute | solution.py:15
  220.6 34.2 %all-reduce.22.cloned.1.call-done = f32[2,128,128]{2,1,0:T(8,128)} async-done(((f32[2,128,128]{2,1,0:T(8,128)}), f32[2,128,128]{2,1,0:T(8,128)}) %all-reduce.22.cloned.1.call-update) | async-done | bytes 131088 | tf_op jit(solution)/shard_map/psum | solution.py:162
  (379 shorter events, 93.8 us)
Async XLA Ops:
  7.2 247.6 %all-reduce.22.cloned.1.call-start = ((), (), s32[]{:S(2)}) async-start(), calls=%async_computation | async-start | bytes 262144 | tf_op jit(solution)/shard_map/psum | solution.py:162
  8.0 27.7 %collective-permute-start = (f32[4,1,128,128]{3,2,1,0:T(8,128)}, f32[4,1,128,128]{3,2,1,0:T(8,128)}, u32[]{:S(2)}, u32[]{:S(2)}) collective-permute-start(f32[4,1,128,128]{3,2,1,0:T(8,128)} %broadcast.302), channel_id=1, source_target_pairs={{4,0},{8,4},{12,8},{5,1},{9,5},{13,9},{6,2},{10,6},{14,10},{7,3},{... | collective-permute-start | bytes 786440 | tf_op jit(solution)/shard_map/ppermute | solution.py:17
  9.4 25.2 %collective-permute-start.1 = (f32[4,1,128,128]{3,2,1,0:T(8,128)}, f32[4,1,128,128]{3,2,1,0:T(8,128)}, u32[]{:S(2)}, u32[]{:S(2)}) collective-permute-start(f32[4,1,128,128]{3,2,1,0:T(8,128)} %broadcast.302), channel_id=1, source_target_pairs={{0,4},{4,8},{8,12},{1,5},{5,9},{9,13},{2,6},{6,10},{10,14},{3,7},{... | collective-permute-start | bytes 786440 | tf_op jit(solution)/shard_map/ppermute | solution.py:15
  15.0 13.9 %collective-permute-start.2 = (bf16[8,1,128,128]{3,2,1,0:T(8,128)(2,1)}, bf16[8,1,128,128]{3,2,1,0:T(8,128)(2,1)}, u32[]{:S(2)}, u32[]{:S(2)}) collective-permute-start(bf16[8,1,128,128]{3,2,1,0:T(8,128)(2,1)} %get-tuple-element.84), channel_id=1, source_target_pairs={{0,4},{4,8},{8,12},{1,5},{5,9},{9,13},{2,6},{6,10},{10,14},{3,7},{... | collective-permute-start | bytes 786440 | tf_op jit(solution)/shard_map/ppermute | solution.py:15
  19.5 10.5 %collective-permute-start.3 = (bf16[8,1,128,128]{3,2,1,0:T(8,128)(2,1)}, bf16[8,1,128,128]{3,2,1,0:T(8,128)(2,1)}, u32[]{:S(2)}, u32[]{:S(2)}) collective-permute-start(bf16[8,1,128,128]{3,2,1,0:T(8,128)(2,1)} %get-tuple-element.83), channel_id=1, source_target_pairs={{4,0},{8,4},{12,8},{5,1},{9,5},{13,9},{6,2},{10,6},{14,10},{7,3},{... | collective-permute-start | bytes 786440 | tf_op jit(solution)/shard_map/ppermute | solution.py:17
  39.8 5.3 %collective-permute-start.4 = (f32[4,1,128,128]{3,2,1,0:T(8,128)S(1)}, f32[4,1,128,128]{3,2,1,0:T(8,128)S(1)}, u32[]{:S(2)}, u32[]{:S(2)}) collective-permute-start(f32[4,1,128,128]{3,2,1,0:T(8,128)S(1)} %get-tuple-element.82), channel_id=1, source_target_pairs={{4,0},{8,4},{12,8},{5,1},{9,5},{13,9},{6,2},{10,6},{14,10},{7,3},{... | collective-permute-start | bytes 786440 | tf_op jit(solution)/shard_map/ppermute | solution.py:17
  48.1 8.0 %collective-permute-start.6 = (f32[4,1,128,128]{3,2,1,0:T(8,128)S(1)}, f32[4,1,128,128]{3,2,1,0:T(8,128)S(1)}, u32[]{:S(2)}, u32[]{:S(2)}) collective-permute-start(f32[4,1,128,128]{3,2,1,0:T(8,128)S(1)} %get-tuple-element.80), channel_id=1, source_target_pairs={{4,0},{8,4},{12,8},{5,1},{9,5},{13,9},{6,2},{10,6},{14,10},{7,3},{... | collective-permute-start | bytes 786440 | tf_op jit(solution)/shard_map/ppermute | solution.py:17
  49.5 7.6 %collective-permute-start.7 = (f32[4,1,128,128]{3,2,1,0:T(8,128)S(1)}, f32[4,1,128,128]{3,2,1,0:T(8,128)S(1)}, u32[]{:S(2)}, u32[]{:S(2)}) collective-permute-start(f32[4,1,128,128]{3,2,1,0:T(8,128)S(1)} %get-tuple-element.79), channel_id=1, source_target_pairs={{0,4},{4,8},{8,12},{1,5},{5,9},{9,13},{2,6},{6,10},{10,14},{3,7},{... | collective-permute-start | bytes 786440 | tf_op jit(solution)/shard_map/ppermute | solution.py:15
  59.1 8.1 %collective-permute-start.9 = (f32[4,1,128,128]{3,2,1,0:T(8,128)S(1)}, f32[4,1,128,128]{3,2,1,0:T(8,128)S(1)}, u32[]{:S(2)}, u32[]{:S(2)}) collective-permute-start(f32[4,1,128,128]{3,2,1,0:T(8,128)S(1)} %get-tuple-element.77), channel_id=1, source_target_pairs={{0,4},{4,8},{8,12},{1,5},{5,9},{9,13},{2,6},{6,10},{10,14},{3,7},{... | collective-permute-start | bytes 786440 | tf_op jit(solution)/shard_map/ppermute | solution.py:15
  65.8 5.4 %collective-permute-start.8 = (f32[4,1,128,128]{3,2,1,0:T(8,128)S(1)}, f32[4,1,128,128]{3,2,1,0:T(8,128)S(1)}, u32[]{:S(2)}, u32[]{:S(2)}) collective-permute-start(f32[4,1,128,128]{3,2,1,0:T(8,128)S(1)} %get-tuple-element.78), channel_id=1, source_target_pairs={{4,0},{8,4},{12,8},{5,1},{9,5},{13,9},{6,2},{10,6},{14,10},{7,3},{... | collective-permute-start | bytes 786440 | tf_op jit(solution)/shard_map/ppermute | solution.py:17
  73.2 8.4 %collective-permute-start.11 = (f32[4,1,128,128]{3,2,1,0:T(8,128)S(1)}, f32[4,1,128,128]{3,2,1,0:T(8,128)S(1)}, u32[]{:S(2)}, u32[]{:S(2)}) collective-permute-start(f32[4,1,128,128]{3,2,1,0:T(8,128)S(1)} %get-tuple-element.75), channel_id=1, source_target_pairs={{0,4},{4,8},{8,12},{1,5},{5,9},{9,13},{2,6},{6,10},{10,14},{3,7},{... | collective-permute-start | bytes 786440 | tf_op jit(solution)/shard_map/ppermute | solution.py:15
  85.6 8.0 %collective-permute-start.13 = (f32[4,1,128,128]{3,2,1,0:T(8,128)S(1)}, f32[4,1,128,128]{3,2,1,0:T(8,128)S(1)}, u32[]{:S(2)}, u32[]{:S(2)}) collective-permute-start(f32[4,1,128,128]{3,2,1,0:T(8,128)S(1)} %get-tuple-element.73), channel_id=1, source_target_pairs={{0,4},{4,8},{8,12},{1,5},{5,9},{9,13},{2,6},{6,10},{10,14},{3,7},{... | collective-permute-start | bytes 786440 | tf_op jit(solution)/shard_map/ppermute | solution.py:15
  97.5 7.7 %collective-permute-start.15 = (f32[4,1,128,128]{3,2,1,0:T(8,128)S(1)}, f32[4,1,128,128]{3,2,1,0:T(8,128)S(1)}, u32[]{:S(2)}, u32[]{:S(2)}) collective-permute-start(f32[4,1,128,128]{3,2,1,0:T(8,128)S(1)} %get-tuple-element.71), channel_id=1, source_target_pairs={{0,4},{4,8},{8,12},{1,5},{5,9},{9,13},{2,6},{6,10},{10,14},{3,7},{... | collective-permute-start | bytes 786440 | tf_op jit(solution)/shard_map/ppermute | solution.py:15
  109.2 7.9 %collective-permute-start.17 = (f32[4,1,128,128]{3,2,1,0:T(8,128)S(1)}, f32[4,1,128,128]{3,2,1,0:T(8,128)S(1)}, u32[]{:S(2)}, u32[]{:S(2)}) collective-permute-start(f32[4,1,128,128]{3,2,1,0:T(8,128)S(1)} %get-tuple-element.69), channel_id=1, source_target_pairs={{0,4},{4,8},{8,12},{1,5},{5,9},{9,13},{2,6},{6,10},{10,14},{3,7},{... | collective-permute-start | bytes 786440 | tf_op jit(solution)/shard_map/ppermute | solution.py:15
  121.1 12.7 %collective-permute-start.18 = (f32[4,2,128,128]{3,2,1,0:T(8,128)S(1)}, f32[4,2,128,128]{3,2,1,0:T(8,128)S(1)}, u32[]{:S(2)}, u32[]{:S(2)}) collective-permute-start(f32[4,2,128,128]{3,2,1,0:T(8,128)S(1)} %pad_maximum_fusion.2), channel_id=1, source_target_pairs={{0,3},{1,0},{2,1},{3,2},{4,7},{5,4},{6,5},{7,6},{8,11},{9,8},{10,9... | collective-permute-start | bytes 1572872 | tf_op jit(solution)/shard_map/ppermute | solution.py:27
  133.8 6.7 %collective-permute-start.20 = (f32[4,1,128,128]{3,2,1,0:T(8,128)S(1)}, f32[4,1,128,128]{3,2,1,0:T(8,128)S(1)}, u32[]{:S(2)}, u32[]{:S(2)}) collective-permute-start(f32[4,1,128,128]{3,2,1,0:T(8,128)S(1)} %get-tuple-element.51), channel_id=1, source_target_pairs={{0,4},{4,8},{8,12},{1,5},{5,9},{9,13},{2,6},{6,10},{10,14},{3,7},{... | collective-permute-start | bytes 786440 | tf_op jit(solution)/shard_map/ppermute | solution.py:15
  144.1 7.5 %collective-permute-start.22 = (f32[4,1,128,128]{3,2,1,0:T(8,128)S(1)}, f32[4,1,128,128]{3,2,1,0:T(8,128)S(1)}, u32[]{:S(2)}, u32[]{:S(2)}) collective-permute-start(f32[4,1,128,128]{3,2,1,0:T(8,128)S(1)} %get-tuple-element.49), channel_id=1, source_target_pairs={{0,4},{4,8},{8,12},{1,5},{5,9},{9,13},{2,6},{6,10},{10,14},{3,7},{... | collective-permute-start | bytes 786440 | tf_op jit(solution)/shard_map/ppermute | solution.py:15
  155.3 7.5 %collective-permute-start.24 = (f32[4,1,128,128]{3,2,1,0:T(8,128)S(1)}, f32[4,1,128,128]{3,2,1,0:T(8,128)S(1)}, u32[]{:S(2)}, u32[]{:S(2)}) collective-permute-start(f32[4,1,128,128]{3,2,1,0:T(8,128)S(1)} %get-tuple-element.47), channel_id=1, source_target_pairs={{0,4},{4,8},{8,12},{1,5},{5,9},{9,13},{2,6},{6,10},{10,14},{3,7},{... | collective-permute-start | bytes 786440 | tf_op jit(solution)/shard_map/ppermute | solution.py:15
  166.4 7.7 %collective-permute-start.26 = (f32[4,1,128,128]{3,2,1,0:T(8,128)S(1)}, f32[4,1,128,128]{3,2,1,0:T(8,128)S(1)}, u32[]{:S(2)}, u32[]{:S(2)}) collective-permute-start(f32[4,1,128,128]{3,2,1,0:T(8,128)S(1)} %get-tuple-element.45), channel_id=1, source_target_pairs={{0,4},{4,8},{8,12},{1,5},{5,9},{9,13},{2,6},{6,10},{10,14},{3,7},{... | collective-permute-start | bytes 786440 | tf_op jit(solution)/shard_map/ppermute | solution.py:15
  177.6 7.5 %collective-permute-start.28 = (f32[4,1,128,128]{3,2,1,0:T(8,128)S(1)}, f32[4,1,128,128]{3,2,1,0:T(8,128)S(1)}, u32[]{:S(2)}, u32[]{:S(2)}) collective-permute-start(f32[4,1,128,128]{3,2,1,0:T(8,128)S(1)} %get-tuple-element.43), channel_id=1, source_target_pairs={{0,4},{4,8},{8,12},{1,5},{5,9},{9,13},{2,6},{6,10},{10,14},{3,7},{... | collective-permute-start | bytes 786440 | tf_op jit(solution)/shard_map/ppermute | solution.py:15
  188.7 7.5 %collective-permute-start.30 = (f32[4,1,128,128]{3,2,1,0:T(8,128)S(1)}, f32[4,1,128,128]{3,2,1,0:T(8,128)S(1)}, u32[]{:S(2)}, u32[]{:S(2)}) collective-permute-start(f32[4,1,128,128]{3,2,1,0:T(8,128)S(1)} %get-tuple-element.41), channel_id=1, source_target_pairs={{0,4},{4,8},{8,12},{1,5},{5,9},{9,13},{2,6},{6,10},{10,14},{3,7},{... | collective-permute-start | bytes 786440 | tf_op jit(solution)/shard_map/ppermute | solution.py:15
  199.8 7.5 %collective-permute-start.32 = (f32[4,1,128,128]{3,2,1,0:T(8,128)S(1)}, f32[4,1,128,128]{3,2,1,0:T(8,128)S(1)}, u32[]{:S(2)}, u32[]{:S(2)}) collective-permute-start(f32[4,1,128,128]{3,2,1,0:T(8,128)S(1)} %get-tuple-element.39), channel_id=1, source_target_pairs={{0,4},{4,8},{8,12},{1,5},{5,9},{9,13},{2,6},{6,10},{10,14},{3,7},{... | collective-permute-start | bytes 786440 | tf_op jit(solution)/shard_map/ppermute | solution.py:15
  213.1 43.1 %collective-permute-start.34 = (f32[4,1,128,128]{3,2,1,0:T(8,128)S(1)}, f32[4,1,128,128]{3,2,1,0:T(8,128)S(1)}, u32[]{:S(2)}, u32[]{:S(2)}) collective-permute-start(f32[4,1,128,128]{3,2,1,0:T(8,128)S(1)} %get-tuple-element.37), channel_id=1, source_target_pairs={{0,4},{4,8},{8,12},{1,5},{5,9},{9,13},{2,6},{6,10},{10,14},{3,7},{... | collective-permute-start | bytes 786440 | tf_op jit(solution)/shard_map/ppermute | solution.py:15
  219.3 36.9 %collective-permute-start.33 = (f32[4,1,128,128]{3,2,1,0:T(8,128)S(1)}, f32[4,1,128,128]{3,2,1,0:T(8,128)S(1)}, u32[]{:S(2)}, u32[]{:S(2)}) collective-permute-start(f32[4,1,128,128]{3,2,1,0:T(8,128)S(1)} %get-tuple-element.38), channel_id=1, source_target_pairs={{4,0},{8,4},{12,8},{5,1},{9,5},{13,9},{6,2},{10,6},{14,10},{7,3},{... | collective-permute-start | bytes 786440 | tf_op jit(solution)/shard_map/ppermute | solution.py:17
  (71 other events, 174.1 us)
Sparse Core Ops, SparseCore 0:
  219.4 35.3 all-reduce.21
where the time goes:
time: 267 us; the launch traced here: 266 us
  starting transfers between devices  125 us (47%)
  waiting for transfers between devices  71 us (27%)
  other arithmetic  37.5 us (14%)
  local copies, waits for them, and re-layouts  16.4 us (6%)
  between operations  16.1 us (6%)
    ppermute x17, starting transfers between devices, padded(): lax.ppermute(tail, axis, [(i, (i + 1) % count) for i in range(ends)])  99 us
    psum x1, waiting for transfers between devices, body(): summed = lax.psum(partial_sum, 'arc')  34.2 us
    ppermute x17, waiting for transfers between devices, padded(): lax.ppermute(head, axis, [((i + 1) % count, i) for i in range(ends)])  26 us
    ppermute x17, starting transfers between devices, padded(): lax.ppermute(head, axis, [((i + 1) % count, i) for i in range(ends)])  22.3 us
    ppermute x1, waiting for transfers between devices, passed_along(): return lax.ppermute(value, axis, pairs)  9.02 us
    concatenate x16, other arithmetic, padded(): jnp.concatenate([lax.ppermute(tail, axis, [(i, (i + 1) % count) for i in...  8.71 us
    unnamed x120, local copies, waits for them, and re-layouts  8.05 us
    add x14, other arithmetic, adjoint_update(): a_now + 0.1 * (1.2 * laplace(ext_a) + carry_a - alpha * a_now - current_a...  7.44 us
  transfers between devices with their start and end apart: 36, of which 16 were waited for; matrix products, arithmetic and copies ran while one was open for 7% of the time, Pallas kernels for 0%

commit v1 on v0

--- a/solution.py
+++ b/solution.py
@@ -2,6 +2,8 @@
 import jax.numpy as jnp
 from jax import lax
 from jax.sharding import PartitionSpec as P
+
+define_gates = lambda which_axis, my_tile: jnp.sum(jax.lax.all_gather(my_tile, which_axis), 0)
 
 
 def padded(cells, sides, width):
@@ -159,7 +161,7 @@
     for interior_block in range(device_instant_total - 1, -1, -1):
         adj, summand_contribution = one_step(adj, interior_block)
         partial_sum = partial_sum + summand_contribution
-    summed = lax.psum(partial_sum, "arc")
+    summed = define_gates("arc", partial_sum)
     share = summed.shape[1] // lax.axis_size("arc")
     gradient = lax.dynamic_slice_in_dim(summed, lax.axis_index("arc") * share, share, 1)
     return (gradient, adj[None])

time: 267 us -> 242 us (0.906)
  waiting for transfers between devices: 71 us -> 36.2 us
  blocking collectives: 0 us -> 16.9 us
  between operations: 16.1 us -> 2.85 us
  other arithmetic: 37.5 us -> 42 us
    psum x1 -> x0, waiting for transfers between devices: 34.2 us -> none  [body(): summed = lax.psum(partial_sum, 'arc')]
    all_gather x0 -> x1, blocking collectives: none -> 16.9 us  [jax.lax.all_gather(my_tile, which_axis)]
    unnamed x120 -> x162, local copies, waits for them, and re-layouts: 8.05 us -> 9.56 us
  transfers between devices with their start and end apart: 36 -> 35, of which waited for: 16 -> 15; matrix products, arithmetic and copies ran while one was open for 7% -> 7% of each run, Pallas kernels for 0% -> 0%
where the time goes in v1:
time: 242 us; the launch traced here: 241 us
  starting transfers between devices  126 us (52%)
  other arithmetic  42 us (17%)
  waiting for transfers between devices  36.2 us (15%)
  local copies, waits for them, and re-layouts  17.1 us (7%)
  blocking collectives  16.9 us (7%)
  between operations  2.85 us (1%)
    ppermute x17, starting transfers between devices, padded(): lax.ppermute(tail, axis, [(i, (i + 1) % count) for i in range(ends)])  99.5 us
    ppermute x17, waiting for transfers between devices, padded(): lax.ppermute(head, axis, [((i + 1) % count, i) for i in range(ends)])  25.4 us
    ppermute x17, starting transfers between devices, padded(): lax.ppermute(head, axis, [((i + 1) % count, i) for i in range(ends)])  22.5 us
    all_gather x1, blocking collectives, jax.lax.all_gather(my_tile, which_axis)  16.9 us
    concatenate x16, other arithmetic, padded(): jnp.concatenate([lax.ppermute(tail, axis, [(i, (i + 1) % count) for i in...  9.86 us
    unnamed x162, local copies, waits for them, and re-layouts  9.56 us
    ppermute x1, waiting for transfers between devices, passed_along(): return lax.ppermute(value, axis, pairs)  9.02 us
    add x14, other arithmetic, adjoint_update(): a_now + 0.1 * (1.2 * laplace(ext_a) + carry_a - alpha * a_now - current_a...  7.47 us
  transfers between devices with their start and end apart: 35, of which 15 were waited for; matrix products, arithmetic and copies ran while one was open for 7% of the time, Pallas kernels for 0%

profile of v1, /device:TPU:0, one launch (start us, length us, event | category | flops | bytes accessed | tf_op | source)
XLA Modules:
  0.0 240.7 jit_solution(7011193559931998268)
XLA Ops:
  2.8 3.7 %collective-permute-start.1 = (f32[4,1,128,128]{3,2,1,0:T(8,128)}, f32[4,1,128,128]{3,2,1,0:T(8,128)}, u32[]{:S(2)}, u32[]{:S(2)}) collective-permute-start(f32[4,1,128,128]{3,2,1,0:T(8,128)} %broadcast.302), channel_id=1, source_target_pairs={{0,4},{4,8},{8,12},{1,5},{5,9},{9,13},{2,6},{6,10},{10,14},{3,7},{... | collective-permute-start | bytes 786440 | tf_op jit(solution)/shard_map/ppermute | solution.py:17
  8.4 4.5 %collective-permute-start.2 = (bf16[8,1,128,128]{3,2,1,0:T(8,128)(2,1)}, bf16[8,1,128,128]{3,2,1,0:T(8,128)(2,1)}, u32[]{:S(2)}, u32[]{:S(2)}) collective-permute-start(bf16[8,1,128,128]{3,2,1,0:T(8,128)(2,1)} %get-tuple-element.84), channel_id=1, source_target_pairs={{0,4},{4,8},{8,12},{1,5},{5,9},{9,13},{2,6},{6,10},{10,14},{3,7},{... | collective-permute-start | bytes 786440 | tf_op jit(solution)/shard_map/ppermute | solution.py:17
  35.1 3.7 %collective-permute-start.5 = (f32[4,1,128,128]{3,2,1,0:T(8,128)S(1)}, f32[4,1,128,128]{3,2,1,0:T(8,128)S(1)}, u32[]{:S(2)}, u32[]{:S(2)}) collective-permute-start(f32[4,1,128,128]{3,2,1,0:T(8,128)S(1)} %get-tuple-element.81), channel_id=1, source_target_pairs={{0,4},{4,8},{8,12},{1,5},{5,9},{9,13},{2,6},{6,10},{10,14},{3,7},{... | collective-permute-start | bytes 786440 | tf_op jit(solution)/shard_map/ppermute | solution.py:17
  43.5 6.4 %collective-permute-start.7 = (f32[4,1,128,128]{3,2,1,0:T(8,128)S(1)}, f32[4,1,128,128]{3,2,1,0:T(8,128)S(1)}, u32[]{:S(2)}, u32[]{:S(2)}) collective-permute-start(f32[4,1,128,128]{3,2,1,0:T(8,128)S(1)} %get-tuple-element.79), channel_id=1, source_target_pairs={{0,4},{4,8},{8,12},{1,5},{5,9},{9,13},{2,6},{6,10},{10,14},{3,7},{... | collective-permute-start | bytes 786440 | tf_op jit(solution)/shard_map/ppermute | solution.py:17
  53.1 6.6 %collective-permute-start.9 = (f32[4,1,128,128]{3,2,1,0:T(8,128)S(1)}, f32[4,1,128,128]{3,2,1,0:T(8,128)S(1)}, u32[]{:S(2)}, u32[]{:S(2)}) collective-permute-start(f32[4,1,128,128]{3,2,1,0:T(8,128)S(1)} %get-tuple-element.77), channel_id=1, source_target_pairs={{0,4},{4,8},{8,12},{1,5},{5,9},{9,13},{2,6},{6,10},{10,14},{3,7},{... | collective-permute-start | bytes 786440 | tf_op jit(solution)/shard_map/ppermute | solution.py:17
  61.2 3.9 %collective-permute-done.8 = f32[4,1,128,128]{3,2,1,0:T(8,128)S(1)} collective-permute-done((f32[4,1,128,128]{3,2,1,0:T(8,128)S(1)}, f32[4,1,128,128]{3,2,1,0:T(8,128)S(1)}, u32[]{:S(2)}, u32[]{:S(2)}) %collective-permute-start.8) | collective-permute-done | bytes 262176 | tf_op jit(solution)/shard_map/ppermute | solution.py:19
  67.2 6.7 %collective-permute-start.11 = (f32[4,1,128,128]{3,2,1,0:T(8,128)S(1)}, f32[4,1,128,128]{3,2,1,0:T(8,128)S(1)}, u32[]{:S(2)}, u32[]{:S(2)}) collective-permute-start(f32[4,1,128,128]{3,2,1,0:T(8,128)S(1)} %get-tuple-element.75), channel_id=1, source_target_pairs={{0,4},{4,8},{8,12},{1,5},{5,9},{9,13},{2,6},{6,10},{10,14},{3,7},{... | collective-permute-start | bytes 786440 | tf_op jit(solution)/shard_map/ppermute | solution.py:17
  79.5 6.2 %collective-permute-start.13 = (f32[4,1,128,128]{3,2,1,0:T(8,128)S(1)}, f32[4,1,128,128]{3,2,1,0:T(8,128)S(1)}, u32[]{:S(2)}, u32[]{:S(2)}) collective-permute-start(f32[4,1,128,128]{3,2,1,0:T(8,128)S(1)} %get-tuple-element.73), channel_id=1, source_target_pairs={{0,4},{4,8},{8,12},{1,5},{5,9},{9,13},{2,6},{6,10},{10,14},{3,7},{... | collective-permute-start | bytes 786440 | tf_op jit(solution)/shard_map/ppermute | solution.py:17
  91.5 6.2 %collective-permute-start.15 = (f32[4,1,128,128]{3,2,1,0:T(8,128)S(1)}, f32[4,1,128,128]{3,2,1,0:T(8,128)S(1)}, u32[]{:S(2)}, u32[]{:S(2)}) collective-permute-start(f32[4,1,128,128]{3,2,1,0:T(8,128)S(1)} %get-tuple-element.71), channel_id=1, source_target_pairs={{0,4},{4,8},{8,12},{1,5},{5,9},{9,13},{2,6},{6,10},{10,14},{3,7},{... | collective-permute-start | bytes 786440 | tf_op jit(solution)/shard_map/ppermute | solution.py:17
  103.3 6.2 %collective-permute-start.17 = (f32[4,1,128,128]{3,2,1,0:T(8,128)S(1)}, f32[4,1,128,128]{3,2,1,0:T(8,128)S(1)}, u32[]{:S(2)}, u32[]{:S(2)}) collective-permute-start(f32[4,1,128,128]{3,2,1,0:T(8,128)S(1)} %get-tuple-element.69), channel_id=1, source_target_pairs={{0,4},{4,8},{8,12},{1,5},{5,9},{9,13},{2,6},{6,10},{10,14},{3,7},{... | collective-permute-start | bytes 786440 | tf_op jit(solution)/shard_map/ppermute | solution.py:17
  115.1 3.7 %collective-permute-start.18 = (f32[4,2,128,128]{3,2,1,0:T(8,128)S(1)}, f32[4,2,128,128]{3,2,1,0:T(8,128)S(1)}, u32[]{:S(2)}, u32[]{:S(2)}) collective-permute-start(f32[4,2,128,128]{3,2,1,0:T(8,128)S(1)} %pad_maximum_fusion.2), channel_id=1, source_target_pairs={{0,3},{1,0},{2,1},{3,2},{4,7},{5,4},{6,5},{7,6},{8,11},{9,8},{10,9... | collective-permute-start | bytes 1572872 | tf_op jit(solution)/shard_map/ppermute | solution.py:29
  118.8 9.0 %collective-permute-done.18 = f32[4,2,128,128]{3,2,1,0:T(8,128)S(1)} collective-permute-done((f32[4,2,128,128]{3,2,1,0:T(8,128)S(1)}, f32[4,2,128,128]{3,2,1,0:T(8,128)S(1)}, u32[]{:S(2)}, u32[]{:S(2)}) %collective-permute-start.18) | collective-permute-done | bytes 524320 | tf_op jit(solution)/shard_map/ppermute | solution.py:29
  127.9 5.3 %collective-permute-start.20 = (f32[4,1,128,128]{3,2,1,0:T(8,128)S(1)}, f32[4,1,128,128]{3,2,1,0:T(8,128)S(1)}, u32[]{:S(2)}, u32[]{:S(2)}) collective-permute-start(f32[4,1,128,128]{3,2,1,0:T(8,128)S(1)} %get-tuple-element.51), channel_id=1, source_target_pairs={{0,4},{4,8},{8,12},{1,5},{5,9},{9,13},{2,6},{6,10},{10,14},{3,7},{... | collective-permute-start | bytes 786440 | tf_op jit(solution)/shard_map/ppermute | solution.py:17
  138.2 6.2 %collective-permute-start.22 = (f32[4,1,128,128]{3,2,1,0:T(8,128)S(1)}, f32[4,1,128,128]{3,2,1,0:T(8,128)S(1)}, u32[]{:S(2)}, u32[]{:S(2)}) collective-permute-start(f32[4,1,128,128]{3,2,1,0:T(8,128)S(1)} %get-tuple-element.49), channel_id=1, source_target_pairs={{0,4},{4,8},{8,12},{1,5},{5,9},{9,13},{2,6},{6,10},{10,14},{3,7},{... | collective-permute-start | bytes 786440 | tf_op jit(solution)/shard_map/ppermute | solution.py:17
  145.7 2.1 collective-permute-done.21
  149.3 6.2 %collective-permute-start.24 = (f32[4,1,128,128]{3,2,1,0:T(8,128)S(1)}, f32[4,1,128,128]{3,2,1,0:T(8,128)S(1)}, u32[]{:S(2)}, u32[]{:S(2)}) collective-permute-start(f32[4,1,128,128]{3,2,1,0:T(8,128)S(1)} %get-tuple-element.47), channel_id=1, source_target_pairs={{0,4},{4,8},{8,12},{1,5},{5,9},{9,13},{2,6},{6,10},{10,14},{3,7},{... | collective-permute-start | bytes 786440 | tf_op jit(solution)/shard_map/ppermute | solution.py:17
  156.8 2.1 collective-permute-done.23
  160.5 6.2 %collective-permute-start.26 = (f32[4,1,128,128]{3,2,1,0:T(8,128)S(1)}, f32[4,1,128,128]{3,2,1,0:T(8,128)S(1)}, u32[]{:S(2)}, u32[]{:S(2)}) collective-permute-start(f32[4,1,128,128]{3,2,1,0:T(8,128)S(1)} %get-tuple-element.45), channel_id=1, source_target_pairs={{0,4},{4,8},{8,12},{1,5},{5,9},{9,13},{2,6},{6,10},{10,14},{3,7},{... | collective-permute-start | bytes 786440 | tf_op jit(solution)/shard_map/ppermute | solution.py:17
  171.6 6.2 %collective-permute-start.28 = (f32[4,1,128,128]{3,2,1,0:T(8,128)S(1)}, f32[4,1,128,128]{3,2,1,0:T(8,128)S(1)}, u32[]{:S(2)}, u32[]{:S(2)}) collective-permute-start(f32[4,1,128,128]{3,2,1,0:T(8,128)S(1)} %get-tuple-element.43), channel_id=1, source_target_pairs={{0,4},{4,8},{8,12},{1,5},{5,9},{9,13},{2,6},{6,10},{10,14},{3,7},{... | collective-permute-start | bytes 786440 | tf_op jit(solution)/shard_map/ppermute | solution.py:17
  182.8 6.3 %collective-permute-start.30 = (f32[4,1,128,128]{3,2,1,0:T(8,128)S(1)}, f32[4,1,128,128]{3,2,1,0:T(8,128)S(1)}, u32[]{:S(2)}, u32[]{:S(2)}) collective-permute-start(f32[4,1,128,128]{3,2,1,0:T(8,128)S(1)} %get-tuple-element.41), channel_id=1, source_target_pairs={{0,4},{4,8},{8,12},{1,5},{5,9},{9,13},{2,6},{6,10},{10,14},{3,7},{... | collective-permute-start | bytes 786440 | tf_op jit(solution)/shard_map/ppermute | solution.py:17
  195.6 6.9 %collective-permute-start.32 = (f32[4,1,128,128]{3,2,1,0:T(8,128)}, f32[4,1,128,128]{3,2,1,0:T(8,128)}, u32[]{:S(2)}, u32[]{:S(2)}) collective-permute-start(f32[4,1,128,128]{3,2,1,0:T(8,128)} %get-tuple-element.39), channel_id=1, source_target_pairs={{0,4},{4,8},{8,12},{1,5},{5,9},{9,13},{2,6},{6,10},{10,14},{3,7},{... | collective-permute-start | bytes 786440 | tf_op jit(solution)/shard_map/ppermute | solution.py:17
  209.1 2.2 fusion.10
  213.4 6.1 %collective-permute-start.34 = (f32[4,1,128,128]{3,2,1,0:T(8,128)S(1)}, f32[4,1,128,128]{3,2,1,0:T(8,128)S(1)}, u32[]{:S(2)}, u32[]{:S(2)}) collective-permute-start(f32[4,1,128,128]{3,2,1,0:T(8,128)S(1)} %get-tuple-element.37), channel_id=1, source_target_pairs={{0,4},{4,8},{8,12},{1,5},{5,9},{9,13},{2,6},{6,10},{10,14},{3,7},{... | collective-permute-start | bytes 786440 | tf_op jit(solution)/shard_map/ppermute | solution.py:17
  219.5 16.9 %all-gather = f32[8,128,128]{2,1,0:T(8,128)S(1)} all-gather(f32[2,128,128]{2,1,0:T(8,128)S(1)} %get-tuple-element.10), channel_id=2, replica_groups=mesh['job'=2,'space'=4,'arc'=4] {'arc'}, dimensions={0}, use_global_device_ids=true | all-gather | bytes 655360 | tf_op jit(solution)/shard_map/all_gather | solution.py:6
  (420 shorter events, 98.5 us)
Async XLA Ops:
  1.4 28.3 %collective-permute-start = (f32[4,1,128,128]{3,2,1,0:T(8,128)}, f32[4,1,128,128]{3,2,1,0:T(8,128)}, u32[]{:S(2)}, u32[]{:S(2)}) collective-permute-start(f32[4,1,128,128]{3,2,1,0:T(8,128)} %broadcast.302), channel_id=1, source_target_pairs={{4,0},{8,4},{12,8},{5,1},{9,5},{13,9},{6,2},{10,6},{14,10},{7,3},{... | collective-permute-start | bytes 786440 | tf_op jit(solution)/shard_map/ppermute | solution.py:19
  2.8 25.8 %collective-permute-start.1 = (f32[4,1,128,128]{3,2,1,0:T(8,128)}, f32[4,1,128,128]{3,2,1,0:T(8,128)}, u32[]{:S(2)}, u32[]{:S(2)}) collective-permute-start(f32[4,1,128,128]{3,2,1,0:T(8,128)} %broadcast.302), channel_id=1, source_target_pairs={{0,4},{4,8},{8,12},{1,5},{5,9},{9,13},{2,6},{6,10},{10,14},{3,7},{... | collective-permute-start | bytes 786440 | tf_op jit(solution)/shard_map/ppermute | solution.py:17
  8.4 14.1 %collective-permute-start.2 = (bf16[8,1,128,128]{3,2,1,0:T(8,128)(2,1)}, bf16[8,1,128,128]{3,2,1,0:T(8,128)(2,1)}, u32[]{:S(2)}, u32[]{:S(2)}) collective-permute-start(bf16[8,1,128,128]{3,2,1,0:T(8,128)(2,1)} %get-tuple-element.84), channel_id=1, source_target_pairs={{0,4},{4,8},{8,12},{1,5},{5,9},{9,13},{2,6},{6,10},{10,14},{3,7},{... | collective-permute-start | bytes 786440 | tf_op jit(solution)/shard_map/ppermute | solution.py:17
  12.9 10.6 %collective-permute-start.3 = (bf16[8,1,128,128]{3,2,1,0:T(8,128)(2,1)}, bf16[8,1,128,128]{3,2,1,0:T(8,128)(2,1)}, u32[]{:S(2)}, u32[]{:S(2)}) collective-permute-start(bf16[8,1,128,128]{3,2,1,0:T(8,128)(2,1)} %get-tuple-element.83), channel_id=1, source_target_pairs={{4,0},{8,4},{12,8},{5,1},{9,5},{13,9},{6,2},{10,6},{14,10},{7,3},{... | collective-permute-start | bytes 786440 | tf_op jit(solution)/shard_map/ppermute | solution.py:19
  33.8 5.2 %collective-permute-start.4 = (f32[4,1,128,128]{3,2,1,0:T(8,128)S(1)}, f32[4,1,128,128]{3,2,1,0:T(8,128)S(1)}, u32[]{:S(2)}, u32[]{:S(2)}) collective-permute-start(f32[4,1,128,128]{3,2,1,0:T(8,128)S(1)} %get-tuple-element.82), channel_id=1, source_target_pairs={{4,0},{8,4},{12,8},{5,1},{9,5},{13,9},{6,2},{10,6},{14,10},{7,3},{... | collective-permute-start | bytes 786440 | tf_op jit(solution)/shard_map/ppermute | solution.py:19
  35.1 4.8 %collective-permute-start.5 = (f32[4,1,128,128]{3,2,1,0:T(8,128)S(1)}, f32[4,1,128,128]{3,2,1,0:T(8,128)S(1)}, u32[]{:S(2)}, u32[]{:S(2)}) collective-permute-start(f32[4,1,128,128]{3,2,1,0:T(8,128)S(1)} %get-tuple-element.81), channel_id=1, source_target_pairs={{0,4},{4,8},{8,12},{1,5},{5,9},{9,13},{2,6},{6,10},{10,14},{3,7},{... | collective-permute-start | bytes 786440 | tf_op jit(solution)/shard_map/ppermute | solution.py:17
  42.1 8.0 %collective-permute-start.6 = (f32[4,1,128,128]{3,2,1,0:T(8,128)S(1)}, f32[4,1,128,128]{3,2,1,0:T(8,128)S(1)}, u32[]{:S(2)}, u32[]{:S(2)}) collective-permute-start(f32[4,1,128,128]{3,2,1,0:T(8,128)S(1)} %get-tuple-element.80), channel_id=1, source_target_pairs={{4,0},{8,4},{12,8},{5,1},{9,5},{13,9},{6,2},{10,6},{14,10},{7,3},{... | collective-permute-start | bytes 786440 | tf_op jit(solution)/shard_map/ppermute | solution.py:19
  43.5 7.6 %collective-permute-start.7 = (f32[4,1,128,128]{3,2,1,0:T(8,128)S(1)}, f32[4,1,128,128]{3,2,1,0:T(8,128)S(1)}, u32[]{:S(2)}, u32[]{:S(2)}) collective-permute-start(f32[4,1,128,128]{3,2,1,0:T(8,128)S(1)} %get-tuple-element.79), channel_id=1, source_target_pairs={{0,4},{4,8},{8,12},{1,5},{5,9},{9,13},{2,6},{6,10},{10,14},{3,7},{... | collective-permute-start | bytes 786440 | tf_op jit(solution)/shard_map/ppermute | solution.py:17
  53.1 8.1 %collective-permute-start.9 = (f32[4,1,128,128]{3,2,1,0:T(8,128)S(1)}, f32[4,1,128,128]{3,2,1,0:T(8,128)S(1)}, u32[]{:S(2)}, u32[]{:S(2)}) collective-permute-start(f32[4,1,128,128]{3,2,1,0:T(8,128)S(1)} %get-tuple-element.77), channel_id=1, source_target_pairs={{0,4},{4,8},{8,12},{1,5},{5,9},{9,13},{2,6},{6,10},{10,14},{3,7},{... | collective-permute-start | bytes 786440 | tf_op jit(solution)/shard_map/ppermute | solution.py:17
  59.7 5.4 %collective-permute-start.8 = (f32[4,1,128,128]{3,2,1,0:T(8,128)S(1)}, f32[4,1,128,128]{3,2,1,0:T(8,128)S(1)}, u32[]{:S(2)}, u32[]{:S(2)}) collective-permute-start(f32[4,1,128,128]{3,2,1,0:T(8,128)S(1)} %get-tuple-element.78), channel_id=1, source_target_pairs={{4,0},{8,4},{12,8},{5,1},{9,5},{13,9},{6,2},{10,6},{14,10},{7,3},{... | collective-permute-start | bytes 786440 | tf_op jit(solution)/shard_map/ppermute | solution.py:19
  67.2 8.4 %collective-permute-start.11 = (f32[4,1,128,128]{3,2,1,0:T(8,128)S(1)}, f32[4,1,128,128]{3,2,1,0:T(8,128)S(1)}, u32[]{:S(2)}, u32[]{:S(2)}) collective-permute-start(f32[4,1,128,128]{3,2,1,0:T(8,128)S(1)} %get-tuple-element.75), channel_id=1, source_target_pairs={{0,4},{4,8},{8,12},{1,5},{5,9},{9,13},{2,6},{6,10},{10,14},{3,7},{... | collective-permute-start | bytes 786440 | tf_op jit(solution)/shard_map/ppermute | solution.py:17
  79.5 8.0 %collective-permute-start.13 = (f32[4,1,128,128]{3,2,1,0:T(8,128)S(1)}, f32[4,1,128,128]{3,2,1,0:T(8,128)S(1)}, u32[]{:S(2)}, u32[]{:S(2)}) collective-permute-start(f32[4,1,128,128]{3,2,1,0:T(8,128)S(1)} %get-tuple-element.73), channel_id=1, source_target_pairs={{0,4},{4,8},{8,12},{1,5},{5,9},{9,13},{2,6},{6,10},{10,14},{3,7},{... | collective-permute-start | bytes 786440 | tf_op jit(solution)/shard_map/ppermute | solution.py:17
  91.5 7.7 %collective-permute-start.15 = (f32[4,1,128,128]{3,2,1,0:T(8,128)S(1)}, f32[4,1,128,128]{3,2,1,0:T(8,128)S(1)}, u32[]{:S(2)}, u32[]{:S(2)}) collective-permute-start(f32[4,1,128,128]{3,2,1,0:T(8,128)S(1)} %get-tuple-element.71), channel_id=1, source_target_pairs={{0,4},{4,8},{8,12},{1,5},{5,9},{9,13},{2,6},{6,10},{10,14},{3,7},{... | collective-permute-start | bytes 786440 | tf_op jit(solution)/shard_map/ppermute | solution.py:17
  103.3 7.9 %collective-permute-start.17 = (f32[4,1,128,128]{3,2,1,0:T(8,128)S(1)}, f32[4,1,128,128]{3,2,1,0:T(8,128)S(1)}, u32[]{:S(2)}, u32[]{:S(2)}) collective-permute-start(f32[4,1,128,128]{3,2,1,0:T(8,128)S(1)} %get-tuple-element.69), channel_id=1, source_target_pairs={{0,4},{4,8},{8,12},{1,5},{5,9},{9,13},{2,6},{6,10},{10,14},{3,7},{... | collective-permute-start | bytes 786440 | tf_op jit(solution)/shard_map/ppermute | solution.py:17
  115.1 12.7 %collective-permute-start.18 = (f32[4,2,128,128]{3,2,1,0:T(8,128)S(1)}, f32[4,2,128,128]{3,2,1,0:T(8,128)S(1)}, u32[]{:S(2)}, u32[]{:S(2)}) collective-permute-start(f32[4,2,128,128]{3,2,1,0:T(8,128)S(1)} %pad_maximum_fusion.2), channel_id=1, source_target_pairs={{0,3},{1,0},{2,1},{3,2},{4,7},{5,4},{6,5},{7,6},{8,11},{9,8},{10,9... | collective-permute-start | bytes 1572872 | tf_op jit(solution)/shard_map/ppermute | solution.py:29
  127.9 6.7 %collective-permute-start.20 = (f32[4,1,128,128]{3,2,1,0:T(8,128)S(1)}, f32[4,1,128,128]{3,2,1,0:T(8,128)S(1)}, u32[]{:S(2)}, u32[]{:S(2)}) collective-permute-start(f32[4,1,128,128]{3,2,1,0:T(8,128)S(1)} %get-tuple-element.51), channel_id=1, source_target_pairs={{0,4},{4,8},{8,12},{1,5},{5,9},{9,13},{2,6},{6,10},{10,14},{3,7},{... | collective-permute-start | bytes 786440 | tf_op jit(solution)/shard_map/ppermute | solution.py:17
  138.2 7.5 %collective-permute-start.22 = (f32[4,1,128,128]{3,2,1,0:T(8,128)S(1)}, f32[4,1,128,128]{3,2,1,0:T(8,128)S(1)}, u32[]{:S(2)}, u32[]{:S(2)}) collective-permute-start(f32[4,1,128,128]{3,2,1,0:T(8,128)S(1)} %get-tuple-element.49), channel_id=1, source_target_pairs={{0,4},{4,8},{8,12},{1,5},{5,9},{9,13},{2,6},{6,10},{10,14},{3,7},{... | collective-permute-start | bytes 786440 | tf_op jit(solution)/shard_map/ppermute | solution.py:17
  149.3 7.5 %collective-permute-start.24 = (f32[4,1,128,128]{3,2,1,0:T(8,128)S(1)}, f32[4,1,128,128]{3,2,1,0:T(8,128)S(1)}, u32[]{:S(2)}, u32[]{:S(2)}) collective-permute-start(f32[4,1,128,128]{3,2,1,0:T(8,128)S(1)} %get-tuple-element.47), channel_id=1, source_target_pairs={{0,4},{4,8},{8,12},{1,5},{5,9},{9,13},{2,6},{6,10},{10,14},{3,7},{... | collective-permute-start | bytes 786440 | tf_op jit(solution)/shard_map/ppermute | solution.py:17
  160.5 7.7 %collective-permute-start.26 = (f32[4,1,128,128]{3,2,1,0:T(8,128)S(1)}, f32[4,1,128,128]{3,2,1,0:T(8,128)S(1)}, u32[]{:S(2)}, u32[]{:S(2)}) collective-permute-start(f32[4,1,128,128]{3,2,1,0:T(8,128)S(1)} %get-tuple-element.45), channel_id=1, source_target_pairs={{0,4},{4,8},{8,12},{1,5},{5,9},{9,13},{2,6},{6,10},{10,14},{3,7},{... | collective-permute-start | bytes 786440 | tf_op jit(solution)/shard_map/ppermute | solution.py:17
  171.6 7.5 %collective-permute-start.28 = (f32[4,1,128,128]{3,2,1,0:T(8,128)S(1)}, f32[4,1,128,128]{3,2,1,0:T(8,128)S(1)}, u32[]{:S(2)}, u32[]{:S(2)}) collective-permute-start(f32[4,1,128,128]{3,2,1,0:T(8,128)S(1)} %get-tuple-element.43), channel_id=1, source_target_pairs={{0,4},{4,8},{8,12},{1,5},{5,9},{9,13},{2,6},{6,10},{10,14},{3,7},{... | collective-permute-start | bytes 786440 | tf_op jit(solution)/shard_map/ppermute | solution.py:17
  182.8 7.6 %collective-permute-start.30 = (f32[4,1,128,128]{3,2,1,0:T(8,128)S(1)}, f32[4,1,128,128]{3,2,1,0:T(8,128)S(1)}, u32[]{:S(2)}, u32[]{:S(2)}) collective-permute-start(f32[4,1,128,128]{3,2,1,0:T(8,128)S(1)} %get-tuple-element.41), channel_id=1, source_target_pairs={{0,4},{4,8},{8,12},{1,5},{5,9},{9,13},{2,6},{6,10},{10,14},{3,7},{... | collective-permute-start | bytes 786440 | tf_op jit(solution)/shard_map/ppermute | solution.py:17
  195.6 8.2 %collective-permute-start.32 = (f32[4,1,128,128]{3,2,1,0:T(8,128)}, f32[4,1,128,128]{3,2,1,0:T(8,128)}, u32[]{:S(2)}, u32[]{:S(2)}) collective-permute-start(f32[4,1,128,128]{3,2,1,0:T(8,128)} %get-tuple-element.39), channel_id=1, source_target_pairs={{0,4},{4,8},{8,12},{1,5},{5,9},{9,13},{2,6},{6,10},{10,14},{3,7},{... | collective-permute-start | bytes 786440 | tf_op jit(solution)/shard_map/ppermute | solution.py:17
  212.1 25.0 %collective-permute-start.33 = (f32[4,1,128,128]{3,2,1,0:T(8,128)S(1)}, f32[4,1,128,128]{3,2,1,0:T(8,128)S(1)}, u32[]{:S(2)}, u32[]{:S(2)}) collective-permute-start(f32[4,1,128,128]{3,2,1,0:T(8,128)S(1)} %get-tuple-element.38), channel_id=1, source_target_pairs={{4,0},{8,4},{12,8},{5,1},{9,5},{13,9},{6,2},{10,6},{14,10},{7,3},{... | collective-permute-start | bytes 786440 | tf_op jit(solution)/shard_map/ppermute | solution.py:19
  213.4 23.7 %collective-permute-start.34 = (f32[4,1,128,128]{3,2,1,0:T(8,128)S(1)}, f32[4,1,128,128]{3,2,1,0:T(8,128)S(1)}, u32[]{:S(2)}, u32[]{:S(2)}) collective-permute-start(f32[4,1,128,128]{3,2,1,0:T(8,128)S(1)} %get-tuple-element.37), channel_id=1, source_target_pairs={{0,4},{4,8},{8,12},{1,5},{5,9},{9,13},{2,6},{6,10},{10,14},{3,7},{... | collective-permute-start | bytes 786440 | tf_op jit(solution)/shard_map/ppermute | solution.py:17
  (91 other events, 485.3 us)
